TPU v7x, 32 devices: a whole 2x2x4 slice. The times are simulated.
32 devices in a mesh: dp: 4 (over z), fsdp: 2 (over x), rows: 4 (over y, core).
Axes of the slice: x: 2, y: 2, z: 4, core: 2. Of those that a mesh axis runs over, the one named last changes fastest.
Arguments:
- feature_maps: bfloat16 [8, 16, 32, 1536], P(('dp', 'fsdp'), 'rows'), may hold values from -30 to 30
- dw_kernel: float32 [7, 7, 1536], replicated, may hold values from -0.875 to 0.875
- norm_gain: float32 [1536], replicated, may hold values from 0.5 to 1.5
- w_up: bfloat16 [1536, 6144], P(('dp', 'rows'), 'fsdp'), may hold values from -0.15625 to 0.15625
- w_down: bfloat16 [6144, 1536], P('fsdp', ('dp', 'rows')), may hold values from -0.078125 to 0.078125
- layer_scale: float32 [1536], replicated, may hold values from 0.3 to 1.5
- d_out: bfloat16 [8, 16, 32, 1536], P(('dp', 'fsdp'), 'rows'), may hold values from -20 to 20
Outputs:
- result: bfloat16 [8, 16, 32, 1536], P(('dp', 'fsdp'), 'rows')
- grad_x: bfloat16 [8, 16, 32, 1536], P(('dp', 'fsdp'), 'rows')
- grad_up: float32 [1536, 6144], P(('dp', 'rows'), 'fsdp')
- grad_down: float32 [6144, 1536], P('fsdp', ('dp', 'rows'))
- grad_kernel: float32 [7, 7, 1536], replicated
- grad_gain: float32 [1536], replicated
- grad_scale: float32 [1536], replicated
All inputs are finite; a program needn't handle non-finite values.
Results may differ from a plain program's by a relative error of at most 0.0075.
Values may be sent and summed in bfloat16 or wider, within the bound.
No kernel may reach another device: no remote copies, remote signals or barrier semaphores. Data moves between devices by JAX's collectives and lax.ppermute only.
A program may use at most 128 MiB of HBM per device.

v0:
```python
import math
import jax
import jax.numpy as jnp
from jax import lax
from jax.sharding import PartitionSpec as P

KS = 7
norm_eps = 1e-06
inv_root_two = 1.0 / math.sqrt(2.0)
inv_root_two_pi = 1.0 / math.sqrt(2.0 * math.pi)
contract_rows = (((0,), (0,)), ((), ()))
contract_cols = (((1,), (1,)), ((), ()))


def padded_2(x, sides, width):
    for axis, dim in sides:
        devices, length = (lax.axis_size(axis), x.shape[dim])
        up = [(i, (i + 1) % devices) for i in range(devices - 1)]
        down = [(j, i) for i, j in up]
        last = lax.slice_in_dim(x, length - width, length, axis=dim)
        leading = lax.slice_in_dim(x, 0, width, axis=dim)
        before = lax.ppermute(last, axis, up)
        after = lax.ppermute(leading, axis, down)
        x = jnp.concatenate([before, x, after], axis=dim)
    return x


def gelu_exact(values):
    return 0.5 * values * (1.0 + jax.scipy.special.erf(values * inv_root_two))


def gelu_slope(values):
    cdf_part = 0.5 * (1.0 + jax.scipy.special.erf(values * inv_root_two))
    return cdf_part + values * jnp.exp(-0.5 * values * values) * inv_root_two_pi


def reduce_down(down_part):
    return lax.psum_scatter(down_part, ("dp", "rows"), scatter_dimension=1, tiled=True)


def body(feature_maps, dw_kernel, norm_gain, w_up, w_down, layer_scale, d_out):
    scenes, strip, across, width = feature_maps.shape
    cells = scenes * strip * across
    rimmed = padded_2(feature_maps, (("rows", 1),), 3)
    padded = jnp.pad(rimmed.astype(jnp.float32), ((0, 0), (0, 0), (3, 3), (0, 0)))
    filtered = jnp.zeros(feature_maps.shape, jnp.float32)
    for row_off in range(KS):
        for col_off in range(KS):
            filtered = (
                filtered
                + padded[:, row_off : row_off + strip, col_off : col_off + across, :]
                * dw_kernel[row_off, col_off]
            )
    flat = filtered.reshape(cells, width)
    average = jnp.mean(flat, axis=-1, keepdims=True)
    center = flat - average
    variance = jnp.mean(center * center, axis=-1, keepdims=True)
    rstd = lax.rsqrt(variance + norm_eps)
    normed = center * rstd
    scaled = (normed * norm_gain).astype(jnp.bfloat16)
    gathered = lax.all_gather(scaled, "fsdp", axis=0, tiled=True)
    up_full = lax.all_gather(w_up, ("dp", "rows"), axis=0, tiled=True)
    down_full = lax.all_gather(w_down, ("dp", "rows"), axis=1, tiled=True)
    hidden = jnp.dot(gathered, up_full, preferred_element_type=jnp.float32)
    active = gelu_exact(hidden).astype(jnp.bfloat16)
    mlp_terms = jnp.dot(active, down_full, preferred_element_type=jnp.float32)
    branch = lax.psum_scatter(
        mlp_terms.astype(jnp.bfloat16), "fsdp", scatter_dimension=0, tiled=True
    ).astype(jnp.float32)
    resid = feature_maps.reshape(cells, width).astype(jnp.float32)
    result = (resid + layer_scale * branch).astype(jnp.bfloat16).reshape(feature_maps.shape)
    cotan = d_out.reshape(cells, width).astype(jnp.float32)
    scale_part = jnp.sum(cotan * branch, axis=0)
    back = (cotan * layer_scale).astype(jnp.bfloat16)
    back_all = lax.all_gather(back, "fsdp", axis=0, tiled=True)
    down_part = lax.dot_general(active, back_all, contract_rows, preferred_element_type=jnp.float32)
    slope_in = lax.dot_general(
        back_all, down_full, contract_cols, preferred_element_type=jnp.float32
    )
    hidden_grad = (slope_in * gelu_slope(hidden)).astype(jnp.bfloat16)
    up_part = lax.dot_general(
        gathered, hidden_grad, contract_rows, preferred_element_type=jnp.float32
    )
    norm_terms = lax.dot_general(
        hidden_grad, up_full, contract_cols, preferred_element_type=jnp.float32
    )
    norm_grad = lax.psum_scatter(norm_terms, "fsdp", scatter_dimension=0, tiled=True)
    grad_up = lax.psum_scatter(up_part, ("dp", "rows"), scatter_dimension=0, tiled=True)
    grad_down = reduce_down(down_part)
    gain_part = jnp.sum(norm_grad * normed, axis=0)
    scaled_grad = norm_grad * norm_gain
    conv_grad = rstd * (
        scaled_grad
        - jnp.mean(scaled_grad, axis=-1, keepdims=True)
        - normed * jnp.mean(scaled_grad * normed, axis=-1, keepdims=True)
    )
    conv_grad = conv_grad.reshape(feature_maps.shape)
    grad_rim = padded_2(conv_grad.astype(jnp.bfloat16), (("rows", 1),), 3).astype(conv_grad.dtype)
    grad_pad = jnp.pad(grad_rim, ((0, 0), (0, 0), (3, 3), (0, 0)))
    kernel_rows = []
    back_conv = jnp.zeros(feature_maps.shape, jnp.float32)
    for row_off in range(KS):
        for col_off in range(KS):
            window = padded[:, row_off : row_off + strip, col_off : col_off + across, :]
            kernel_rows.append(jnp.sum(window * conv_grad, axis=(0, 1, 2)))
            back_conv = (
                back_conv
                + grad_pad[
                    :, 6 - row_off : 6 - row_off + strip, 6 - col_off : 6 - col_off + across, :
                ]
                * dw_kernel[row_off, col_off]
            )
    kernel_part = jnp.stack(kernel_rows).reshape(KS, KS, width)
    grad_x = (d_out.astype(jnp.float32) + back_conv).astype(jnp.bfloat16)
    grad_kernel, grad_gain, grad_scale = lax.psum(
        (kernel_part, gain_part, scale_part), ("dp", "fsdp", "rows")
    )
    return (result, grad_x, grad_up, grad_down, grad_kernel, grad_gain, grad_scale)


def solution(mesh):
    return jax.shard_map(
        body,
        mesh=mesh,
        in_specs=(
            P(("dp", "fsdp"), "rows", None, None),
            P(),
            P(),
            P(("dp", "rows"), "fsdp"),
            P("fsdp", ("dp", "rows")),
            P(),
            P(("dp", "fsdp"), "rows", None, None),
        ),
        out_specs=(
            P(("dp", "fsdp"), "rows", None, None),
            P(("dp", "fsdp"), "rows", None, None),
            P(("dp", "rows"), "fsdp"),
            P("fsdp", ("dp", "rows")),
            P(),
            P(),
            P(),
        ),
        check_vma=False,
    )
```

profile of v0, /device:TPU:0, one launch (start us, length us, event | category | flops | bytes accessed | tf_op | source)
XLA Modules:
  0.0 797.9 jit_solution(10668589192870983978)
XLA Ops:
  7.2 0.0 copy-start.9
  7.2 0.0 all-gather.3.cloned.1.call-start
  7.2 0.7 all-gather.3.cloned.1.call-update
  7.9 0.0 all-gather.5.cloned.1.call-start
  8.0 0.7 all-gather.5.cloned.1.call-update
  8.7 0.0 reduce-scatter.5.cloned.1.call-start
  8.7 1.1 fusion.105
  9.8 2.4 collective-permute-start
  12.2 1.3 collective-permute-start.1
  13.5 1.3 slice_reduce_fusion.46
  14.9 0.0 copy-start.27
  14.9 0.3 slice_reduce_fusion.48
  15.5 0.9 slice_reduce_fusion.47
  16.4 1.4 collective-permute-done.1
  17.8 0.1 maximum_convert_fusion
  18.0 9.5 %fusion.103 = (f32[4,32]{1,0:T(4,128)S(1)}, f32[1,4,32,1536]{3,2,1,0:T(8,128)S(1)}) fusion(f32[1536]{0:T(1024)S(1)} %get-tuple-element.106, f32[1536]{0:T(1024)S(1)} %get-tuple-element.107, f32[1536]{0:T(1024)S(1)} %get-tuple-element.60, f32[1536]{0:T(1024)S(1)} %get-tuple-element.61, f32[1,10,32,1536]{3,2,1,0:T(8,128)S(1)} %maximum_convert_fusion, ...), kind=kLoop, calls=%fused_computation.314 | loop fusion | flops 19267456 | bytes 8641024 | tf_op jit(solution)/shard_map/reduce_sum | solution.py:55
  27.8 0.6 div.15
  28.4 0.2 multiply_reduce_fusion.51
  28.6 0.6 rsqrt.12
  29.3 0.8 multiply_convert_fusion.1
  30.1 8.6 %all_gather.12 = bf16[256,1536]{1,0:T(8,128)(2,1)} all-gather(bf16[128,1536]{1,0:T(8,128)(2,1)S(1)} %multiply_convert_fusion.1), channel_id=1, replica_groups=mesh['dp'=4,'fsdp'=2,'rows'=4] {'fsdp'}, dimensions={0}, use_global_device_ids=true | all-gather | bytes 1179648 | tf_op jit(solution)/shard_map/all_gather | solution.py:61
  38.7 55.8 %all-gather.3.cloned.1.call-done = bf16[1536,3072]{1,0:T(8,128)(2,1)} async-done(((bf16[96,3072]{1,0:T(8,128)(2,1)}), bf16[1536,3072]{1,0:T(8,128)(2,1)}) %all-gather.3.cloned.1.call-update) | async-done | bytes 9437200 | tf_op jit(solution)/shard_map/all_gather | solution.py:62
  94.5 8.2 %fusion.106 = f32[256,3072]{1,0:T(8,128)} fusion(bf16[256,1536]{1,0:T(8,128)(2,1)} %all_gather.12, bf16[1536,3072]{1,0:T(8,128)(2,1)} %all-gather.3.cloned.1.call-done), kind=kOutput, calls=%fused_computation.317 | convolution fusion | flops 2415919104 | bytes 13369344 | tf_op jit(solution)/shard_map/dot_general | solution.py:64
  102.7 73.7 %all-gather.5.cloned.1.call-done = bf16[3072,1536]{0,1:T(8,128)(2,1)} async-done(((bf16[3072,96]{0,1:T(8,128)(2,1)}), bf16[3072,1536]{0,1:T(8,128)(2,1)}) %all-gather.5.cloned.1.call-update) | async-done | bytes 9437200 | tf_op jit(solution)/shard_map/all_gather | solution.py:63
  176.4 8.2 %convolution_convert_fusion = bf16[256,1536]{1,0:T(8,128)(2,1)} fusion(bf16[3072,1536]{0,1:T(8,128)(2,1)} %all-gather.5.cloned.1.call-done, f32[256,3072]{1,0:T(8,128)} %fusion.106), kind=kOutput, calls=%fused_computation.93 | convolution fusion | flops 2420244480 | bytes 13369344 | tf_op jit(solution)/shard_map/dot_general | solution.py:66
  184.5 0.0 reduce-scatter.5.cloned.1.call-update
  184.6 0.0 reduce-scatter.7.cloned.1.call-start
  184.6 15.7 %reduce-scatter.5.cloned.1.call-done = bf16[128,1536]{1,0:T(8,128)(2,1)} async-done(((bf16[256,1536]{1,0:T(8,128)(2,1)}), bf16[128,1536]{1,0:T(8,128)(2,1)}) %reduce-scatter.5.cloned.1.call-update) | async-done | bytes 393232 | tf_op jit(solution)/shard_map/reduce_scatter | solution.py:67
  200.3 2.7 fusion.7
  203.0 11.8 %all_gather.15 = bf16[256,1536]{1,0:T(8,128)(2,1)S(1)} all-gather(bf16[128,1536]{1,0:T(8,128)(2,1)S(1)} %get-tuple-element.114), channel_id=1, replica_groups=mesh['dp'=4,'fsdp'=2,'rows'=4] {'fsdp'}, dimensions={0}, use_global_device_ids=true | all-gather | bytes 1179648 | tf_op jit(solution)/shard_map/all_gather | solution.py:75
  214.8 0.9 copy-done.2
  215.7 5.5 fusion
  221.3 1.2 copy-done.7
  222.5 0.0 copy-start.89
  222.5 3.8 fusion.107
  226.3 0.0 reduce-scatter.7.cloned.1.call-update
  226.3 0.0 all-reduce.5.cloned.1.call-start
  226.4 26.2 %reduce-scatter.7.cloned.1.call-done = f32[128,1536]{1,0:T(8,128)} async-done(((f32[256,1536]{1,0:T(8,128)}), f32[128,1536]{1,0:T(8,128)}) %reduce-scatter.7.cloned.1.call-update) | async-done | bytes 786448 | tf_op jit(solution)/shard_map/reduce_scatter | solution.py:87
  252.6 2.0 multiply_reduce_fusion
  254.6 3.6 multiply_reduce_fusion.2
  258.2 1.2 multiply_reduce_fusion.3
  259.4 0.0 copy-start.3
  259.4 2.0 multiply_reduce_fusion.1
  262.1 0.5 stack.199
  262.6 0.8 reshape.323
  263.4 0.0 all-reduce.5.cloned.1.call-update
  263.4 0.0 reduce-scatter.11.cloned.1.call-start
  263.5 11.1 %fusion.102 = f32[3072,1536]{0,1:T(8,128)} fusion(bf16[256,1536]{1,0:T(8,128)(2,1)S(1)} %copy-done.3, f32[256,3072]{1,0:T(8,128)} %fusion.106), kind=kOutput, calls=%fused_computation.313 | convolution fusion | flops 2419851264 | bytes 22806528 | tf_op jit(solution)/shard_map/dot_general | solution.py:76
  274.6 0.0 reduce-scatter.11.cloned.1.call-update
  274.6 0.3 reduce-scatter.9.cloned.1.call-start
  274.9 0.8 copy-done.1
  275.7 0.5 copy-done.8
  276.2 7.9 fusion.108
  284.1 0.0 reduce-scatter.9.cloned.1.call-update
  284.2 0.0 copy-start.6
  284.7 1.9 collective-permute-start.2
  286.5 1.3 collective-permute-start.3
  287.9 42.3 %all-reduce.2 = (f32[1536]{0:T(1024)}, f32[1536]{0:T(1024)}) all-reduce(f32[1536]{0:T(1024)} %get-tuple-element.56, f32[1536]{0:T(1024)} %get-tuple-element.113), channel_id=1, replica_groups=mesh['dp'=4,'fsdp'=2,'rows'=4] {'dp','fsdp','rows'}, use_global_device_ids=true, to_apply=%region_59.60 | all-reduce | flops 3072 | bytes 24576 | tf_op jit(solution)/shard_map/psum | solution.py:115
  330.2 0.1 maximum_convert_fusion.1
  330.7 7.5 fusion.95
  338.3 51.2 %all-reduce.5.cloned.1.call-done = f32[7,7,1536]{2,1,0:T(8,128)} async-done(((f32[7,7,1536]{2,1,0:T(8,128)}), f32[7,7,1536]{2,1,0:T(8,128)}) %all-reduce.5.cloned.1.call-update) | async-done | bytes 301072 | tf_op jit(solution)/shard_map/psum | solution.py:115
  389.4 200.8 %reduce-scatter.11.cloned.1.call-done = f32[3072,96]{0,1:T(8,128)} async-done(((f32[3072,1536]{0,1:T(8,128)}), f32[3072,96]{0,1:T(8,128)}) %reduce-scatter.11.cloned.1.call-update) | async-done | bytes 1179664 | tf_op jit(solution)/shard_map/reduce_scatter | solution.py:38
  590.2 199.1 %reduce-scatter.9.cloned.1.call-done = f32[96,3072]{1,0:T(8,128)} async-done(((f32[1536,3072]{1,0:T(8,128)}), f32[96,3072]{1,0:T(8,128)}) %reduce-scatter.9.cloned.1.call-update) | async-done | bytes 1179664 | tf_op jit(solution)/shard_map/reduce_scatter | solution.py:88
  789.3 1.7 copy.15
  (238 shorter events, 0.8 us)
Async XLA Ops:
  7.2 87.3 %all-gather.3.cloned.1.call-start = ((), (), s32[]{:S(2)}) async-start(), calls=%async_computation.4 | async-start | bytes 10027008 | tf_op jit(solution)/shard_map/all_gather | solution.py:62
  7.9 168.5 %all-gather.5.cloned.1.call-start = ((), (), s32[]{:S(2)}) async-start(), calls=%async_computation.5 | async-start | bytes 10027008 | tf_op jit(solution)/shard_map/all_gather | solution.py:63
  8.7 191.6 %reduce-scatter.5.cloned.1.call-start = ((), (), s32[]{:S(2)}) async-start(), calls=%async_computation.6 | async-start | bytes 1179648 | tf_op jit(solution)/shard_map/reduce_scatter | solution.py:67
  9.8 6.6 collective-permute-start
  12.2 5.6 collective-permute-start.1
  14.8 12.6 %copy-start.11 = (f32[1536]{0:T(1024)}, f32[1536]{0:T(1024)S(1)}, u32[]{:S(2)}) copy-start(f32[1536]{0:T(1024)S(1)} %get-tuple-element.98) | copy-start | bytes 18436
  14.9 12.6 %copy-start.13 = (f32[1536]{0:T(1024)}, f32[1536]{0:T(1024)S(1)}, u32[]{:S(2)}) copy-start(f32[1536]{0:T(1024)S(1)} %get-tuple-element.99) | copy-start | bytes 18436
  14.9 12.6 %copy-start.15 = (f32[1536]{0:T(1024)}, f32[1536]{0:T(1024)S(1)}, u32[]{:S(2)}) copy-start(f32[1536]{0:T(1024)S(1)} %get-tuple-element.100) | copy-start | bytes 18436
  14.9 12.6 %copy-start.17 = (f32[1536]{0:T(1024)}, f32[1536]{0:T(1024)S(1)}, u32[]{:S(2)}) copy-start(f32[1536]{0:T(1024)S(1)} %get-tuple-element.101) | copy-start | bytes 18436
  14.9 12.6 %copy-start.19 = (f32[1536]{0:T(1024)}, f32[1536]{0:T(1024)S(1)}, u32[]{:S(2)}) copy-start(f32[1536]{0:T(1024)S(1)} %get-tuple-element.102) | copy-start | bytes 18436
  14.9 12.6 %copy-start.21 = (f32[1536]{0:T(1024)}, f32[1536]{0:T(1024)S(1)}, u32[]{:S(2)}) copy-start(f32[1536]{0:T(1024)S(1)} %get-tuple-element.103) | copy-start | bytes 18436
  14.9 12.6 %copy-start.23 = (f32[1536]{0:T(1024)}, f32[1536]{0:T(1024)S(1)}, u32[]{:S(2)}) copy-start(f32[1536]{0:T(1024)S(1)} %get-tuple-element.104) | copy-start | bytes 18436
  14.9 12.6 %copy-start.25 = (f32[1536]{0:T(1024)}, f32[1536]{0:T(1024)S(1)}, u32[]{:S(2)}) copy-start(f32[1536]{0:T(1024)S(1)} %get-tuple-element.105) | copy-start | bytes 18436
  102.7 97.6 %copy-start.5 = (bf16[1,4,32,1536]{3,2,1,0:T(8,128)(2,1)S(1)}, bf16[1,4,32,1536]{3,2,1,0:T(8,128)(2,1)}, u32[]{:S(2)}) copy-start(bf16[1,4,32,1536]{3,2,1,0:T(8,128)(2,1)} %param.13) | copy-start | bytes 1179652
  184.6 68.0 %reduce-scatter.7.cloned.1.call-start = ((), (), s32[]{:S(2)}) async-start(), calls=%async_computation.7 | async-start | bytes 2359296 | tf_op jit(solution)/shard_map/reduce_scatter | solution.py:87
  200.3 15.4 %copy-start.4 = (f32[256,3072]{1,0:T(8,128)S(1)}, f32[256,3072]{1,0:T(8,128)}, u32[]{:S(2)}) copy-start(f32[256,3072]{1,0:T(8,128)} %fusion.106) | copy-start | bytes 9437188
  203.0 19.5 %slice-start = ((s8[9437184]{0:T(1024)(128)(4,1)}), s8[4194304]{0:T(1024)(128)(4,1)S(1)}, s32[]{:S(2)}) async-start(s8[9437184]{0:T(1024)(128)(4,1)} %bitcast.86), calls=%async_computation.11 | async-start | bytes 8388608
  222.5 30.1 %copy-start.89 = (f32[128]{0:T(128)S(1)}, f32[128]{0:T(128)}, u32[]{:S(2)}) copy-start(f32[128]{0:T(128)} %div.15) | copy-start | bytes 1540
  222.5 30.1 %copy-start.90 = (f32[128]{0:T(128)S(1)}, f32[128]{0:T(128)}, u32[]{:S(2)}) copy-start(f32[128]{0:T(128)} %rsqrt.12) | copy-start | bytes 1540
  226.3 163.1 %all-reduce.5.cloned.1.call-start = ((), (), s32[]{:S(2)}) async-start(), calls=%async_computation.10 | async-start | bytes 688128 | tf_op jit(solution)/shard_map/psum | solution.py:115
  263.4 326.7 %reduce-scatter.11.cloned.1.call-start = ((), (), s32[]{:S(2)}) async-start(), calls=%async_computation.9 | async-start | bytes 20054016 | tf_op jit(solution)/shard_map/reduce_scatter | solution.py:38
  274.6 514.7 %reduce-scatter.9.cloned.1.call-start = ((), (), s32[]{:S(2)}) async-start(), calls=%async_computation.8 | async-start | bytes 20054016 | tf_op jit(solution)/shard_map/reduce_scatter | solution.py:88
  284.2 46.1 %copy-start.6 = (bf16[1,4,32,1536]{3,2,1,0:T(8,128)(2,1)S(1)}, bf16[1,4,32,1536]{3,2,1,0:T(8,128)(2,1)}, u32[]{:S(2)}) copy-start(bf16[1,4,32,1536]{3,2,1,0:T(8,128)(2,1)} %param.13) | copy-start | bytes 1179652
  284.2 46.1 %copy-start.12 = (f32[1536]{0:T(1024)S(1)}, f32[1536]{0:T(1024)}, u32[]{:S(2)}) copy-start(f32[1536]{0:T(1024)} %copy-done.11) | copy-start | bytes 18436
  284.2 46.1 %copy-start.14 = (f32[1536]{0:T(1024)S(1)}, f32[1536]{0:T(1024)}, u32[]{:S(2)}) copy-start(f32[1536]{0:T(1024)} %copy-done.13) | copy-start | bytes 18436
  284.2 46.1 %copy-start.16 = (f32[1536]{0:T(1024)S(1)}, f32[1536]{0:T(1024)}, u32[]{:S(2)}) copy-start(f32[1536]{0:T(1024)} %copy-done.15) | copy-start | bytes 18436
  284.2 46.1 %copy-start.18 = (f32[1536]{0:T(1024)S(1)}, f32[1536]{0:T(1024)}, u32[]{:S(2)}) copy-start(f32[1536]{0:T(1024)} %copy-done.17) | copy-start | bytes 18436
  284.3 46.1 %copy-start.20 = (f32[1536]{0:T(1024)S(1)}, f32[1536]{0:T(1024)}, u32[]{:S(2)}) copy-start(f32[1536]{0:T(1024)} %copy-done.19) | copy-start | bytes 18436
  284.3 46.1 %copy-start.22 = (f32[1536]{0:T(1024)S(1)}, f32[1536]{0:T(1024)}, u32[]{:S(2)}) copy-start(f32[1536]{0:T(1024)} %copy-done.21) | copy-start | bytes 18436
  284.3 46.1 %copy-start.24 = (f32[1536]{0:T(1024)S(1)}, f32[1536]{0:T(1024)}, u32[]{:S(2)}) copy-start(f32[1536]{0:T(1024)} %copy-done.23) | copy-start | bytes 18436
  284.3 46.1 %copy-start.26 = (f32[1536]{0:T(1024)S(1)}, f32[1536]{0:T(1024)}, u32[]{:S(2)}) copy-start(f32[1536]{0:T(1024)} %copy-done.25) | copy-start | bytes 18436
  284.3 46.1 %copy-start.28 = (f32[1536]{0:T(1024)S(1)}, f32[1536]{0:T(1024)}, u32[]{:S(2)}) copy-start(f32[1536]{0:T(1024)} %copy-done.27) | copy-start | bytes 18436
  284.3 46.1 %copy-start.30 = (f32[1536]{0:T(1024)S(1)}, f32[1536]{0:T(1024)}, u32[]{:S(2)}) copy-start(f32[1536]{0:T(1024)} %copy-done.29) | copy-start | bytes 18436
  284.3 46.1 %copy-start.32 = (f32[1536]{0:T(1024)S(1)}, f32[1536]{0:T(1024)}, u32[]{:S(2)}) copy-start(f32[1536]{0:T(1024)} %copy-done.31) | copy-start | bytes 18436
  284.3 46.1 %copy-start.34 = (f32[1536]{0:T(1024)S(1)}, f32[1536]{0:T(1024)}, u32[]{:S(2)}) copy-start(f32[1536]{0:T(1024)} %copy-done.33) | copy-start | bytes 18436
  284.3 46.1 %copy-start.36 = (f32[1536]{0:T(1024)S(1)}, f32[1536]{0:T(1024)}, u32[]{:S(2)}) copy-start(f32[1536]{0:T(1024)} %copy-done.35) | copy-start | bytes 18436
  284.3 46.1 %copy-start.38 = (f32[1536]{0:T(1024)S(1)}, f32[1536]{0:T(1024)}, u32[]{:S(2)}) copy-start(f32[1536]{0:T(1024)} %copy-done.37) | copy-start | bytes 18436
  284.4 46.1 %copy-start.40 = (f32[1536]{0:T(1024)S(1)}, f32[1536]{0:T(1024)}, u32[]{:S(2)}) copy-start(f32[1536]{0:T(1024)} %copy-done.39) | copy-start | bytes 18436
  284.4 46.1 %copy-start.42 = (f32[1536]{0:T(1024)S(1)}, f32[1536]{0:T(1024)}, u32[]{:S(2)}) copy-start(f32[1536]{0:T(1024)} %copy-done.41) | copy-start | bytes 18436
  284.4 46.1 %copy-start.44 = (f32[1536]{0:T(1024)S(1)}, f32[1536]{0:T(1024)}, u32[]{:S(2)}) copy-start(f32[1536]{0:T(1024)} %copy-done.43) | copy-start | bytes 18436
  284.4 46.1 %copy-start.46 = (f32[1536]{0:T(1024)S(1)}, f32[1536]{0:T(1024)}, u32[]{:S(2)}) copy-start(f32[1536]{0:T(1024)} %copy-done.45) | copy-start | bytes 18436
  284.4 46.1 %copy-start.48 = (f32[1536]{0:T(1024)S(1)}, f32[1536]{0:T(1024)}, u32[]{:S(2)}) copy-start(f32[1536]{0:T(1024)} %copy-done.47) | copy-start | bytes 18436
  284.4 46.1 %copy-start.50 = (f32[1536]{0:T(1024)S(1)}, f32[1536]{0:T(1024)}, u32[]{:S(2)}) copy-start(f32[1536]{0:T(1024)} %copy-done.49) | copy-start | bytes 18436
  284.4 46.1 %copy-start.52 = (f32[1536]{0:T(1024)S(1)}, f32[1536]{0:T(1024)}, u32[]{:S(2)}) copy-start(f32[1536]{0:T(1024)} %copy-done.51) | copy-start | bytes 18436
  284.4 46.1 %copy-start.54 = (f32[1536]{0:T(1024)S(1)}, f32[1536]{0:T(1024)}, u32[]{:S(2)}) copy-start(f32[1536]{0:T(1024)} %copy-done.53) | copy-start | bytes 18436
  284.4 46.1 %copy-start.56 = (f32[1536]{0:T(1024)S(1)}, f32[1536]{0:T(1024)}, u32[]{:S(2)}) copy-start(f32[1536]{0:T(1024)} %copy-done.55) | copy-start | bytes 18436
  284.4 46.1 %copy-start.58 = (f32[1536]{0:T(1024)S(1)}, f32[1536]{0:T(1024)}, u32[]{:S(2)}) copy-start(f32[1536]{0:T(1024)} %copy-done.57) | copy-start | bytes 18436
  284.5 46.1 %copy-start.60 = (f32[1536]{0:T(1024)S(1)}, f32[1536]{0:T(1024)}, u32[]{:S(2)}) copy-start(f32[1536]{0:T(1024)} %copy-done.59) | copy-start | bytes 18436
  284.5 46.1 %copy-start.62 = (f32[1536]{0:T(1024)S(1)}, f32[1536]{0:T(1024)}, u32[]{:S(2)}) copy-start(f32[1536]{0:T(1024)} %copy-done.61) | copy-start | bytes 18436
  284.5 46.1 %copy-start.64 = (f32[1536]{0:T(1024)S(1)}, f32[1536]{0:T(1024)}, u32[]{:S(2)}) copy-start(f32[1536]{0:T(1024)} %copy-done.63) | copy-start | bytes 18436
  284.5 46.1 %copy-start.66 = (f32[1536]{0:T(1024)S(1)}, f32[1536]{0:T(1024)}, u32[]{:S(2)}) copy-start(f32[1536]{0:T(1024)} %copy-done.65) | copy-start | bytes 18436
  284.5 46.1 %copy-start.68 = (f32[1536]{0:T(1024)S(1)}, f32[1536]{0:T(1024)}, u32[]{:S(2)}) copy-start(f32[1536]{0:T(1024)} %copy-done.67) | copy-start | bytes 18436
  284.5 46.1 %copy-start.70 = (f32[1536]{0:T(1024)S(1)}, f32[1536]{0:T(1024)}, u32[]{:S(2)}) copy-start(f32[1536]{0:T(1024)} %copy-done.69) | copy-start | bytes 18436
  284.5 46.1 %copy-start.72 = (f32[1536]{0:T(1024)S(1)}, f32[1536]{0:T(1024)}, u32[]{:S(2)}) copy-start(f32[1536]{0:T(1024)} %copy-done.71) | copy-start | bytes 18436
  284.5 46.1 %copy-start.74 = (f32[1536]{0:T(1024)S(1)}, f32[1536]{0:T(1024)}, u32[]{:S(2)}) copy-start(f32[1536]{0:T(1024)} %copy-done.73) | copy-start | bytes 18436
  284.5 46.1 %copy-start.76 = (f32[1536]{0:T(1024)S(1)}, f32[1536]{0:T(1024)}, u32[]{:S(2)}) copy-start(f32[1536]{0:T(1024)} %copy-done.75) | copy-start | bytes 18436
  284.5 46.1 %copy-start.78 = (f32[1536]{0:T(1024)S(1)}, f32[1536]{0:T(1024)}, u32[]{:S(2)}) copy-start(f32[1536]{0:T(1024)} %copy-done.77) | copy-start | bytes 18436
  284.6 46.1 %copy-start.80 = (f32[1536]{0:T(1024)S(1)}, f32[1536]{0:T(1024)}, u32[]{:S(2)}) copy-start(f32[1536]{0:T(1024)} %copy-done.79) | copy-start | bytes 18436
  284.6 46.1 %copy-start.82 = (f32[1536]{0:T(1024)S(1)}, f32[1536]{0:T(1024)}, u32[]{:S(2)}) copy-start(f32[1536]{0:T(1024)} %copy-done.81) | copy-start | bytes 18436
  284.6 46.1 %copy-start.84 = (f32[1536]{0:T(1024)S(1)}, f32[1536]{0:T(1024)}, u32[]{:S(2)}) copy-start(f32[1536]{0:T(1024)} %copy-done.83) | copy-start | bytes 18436
  284.6 46.1 %copy-start.86 = (f32[1536]{0:T(1024)S(1)}, f32[1536]{0:T(1024)}, u32[]{:S(2)}) copy-start(f32[1536]{0:T(1024)} %copy-done.85) | copy-start | bytes 18436
  284.6 46.1 %copy-start.88 = (f32[1536]{0:T(1024)S(1)}, f32[1536]{0:T(1024)}, u32[]{:S(2)}) copy-start(f32[1536]{0:T(1024)} %copy-done.87) | copy-start | bytes 18436
  284.7 45.5 %collective-permute-start.2 = (bf16[1,3,32,1536]{3,2,1,0:T(8,128)(2,1)S(1)}, bf16[1,3,32,1536]{3,2,1,0:T(8,128)(2,1)S(1)}, u32[]{:S(2)}, u32[]{:S(2)}) collective-permute-start(bf16[1,3,32,1536]{3,2,1,0:T(8,128)(2,1)S(1)} %get-tuple-element.116), channel_id=1, source_target_pairs={{0,1},{1,2},{2,3},{4,5},{5,6},{6,7},{8,9},{9,10},{10,11},{12,13},{... | collective-permute-start | bytes 884744 | tf_op jit(solution)/shard_map/ppermute | solution.py:22
  286.5 43.6 %collective-permute-start.3 = (bf16[1,3,32,1536]{3,2,1,0:T(8,128)(2,1)S(1)}, bf16[1,3,32,1536]{3,2,1,0:T(8,128)(2,1)S(1)}, u32[]{:S(2)}, u32[]{:S(2)}) collective-permute-start(bf16[1,3,32,1536]{3,2,1,0:T(8,128)(2,1)S(1)} %get-tuple-element.117), channel_id=1, source_target_pairs={{1,0},{2,1},{3,2},{5,4},{6,5},{7,6},{9,8},{10,9},{11,10},{13,12},{... | collective-permute-start | bytes 884744 | tf_op jit(solution)/shard_map/ppermute | solution.py:23
  (41 other events, 423.7 us)
Sparse Core Ops, SparseCore 0:
  10.3 84.1 all-gather.2
  96.8 79.5 all-gather.4
  184.7 15.5 reduce-scatter.4
  226.4 26.0 reduce-scatter.6
  263.6 125.8 all-reduce.4
  394.5 195.6 reduce-scatter.10
  595.4 193.8 reduce-scatter.8
where the time goes:
time: 799 us; the launch traced here: 798 us
  waiting for transfers between devices  625 us (78%)
  blocking collectives  62.7 us (8%)
  matrix products  44.7 us (6%)
  other arithmetic  30 us (4%)
  between operations  16 us (2%)
  local copies, waits for them, and re-layouts  12.1 us (2%)
    reduce_scatter x1, waiting for transfers between devices, reduce_down(): lax.psum_scatter(down_part, ('dp', 'rows'), scatter_dimension=1, tiled=True)  201 us
    reduce_scatter x1, waiting for transfers between devices, body(): lax.psum_scatter(up_part, ('dp', 'rows'), scatter_dimension=0, tiled=True)  199 us
    all_gather x1, waiting for transfers between devices, body(): down_full = lax.all_gather(w_down, ('dp', 'rows'), axis=1, tiled=True)  73.7 us
    all_gather x1, waiting for transfers between devices, body(): up_full = lax.all_gather(w_up, ('dp', 'rows'), axis=0, tiled=True)  55.8 us
    psum x1, waiting for transfers between devices, body(): lax.psum((kernel_part, gain_part, scale_part), ('dp', 'fsdp', 'rows'))  51.2 us
    psum x1, blocking collectives, body(): lax.psum((kernel_part, gain_part, scale_part), ('dp', 'fsdp', 'rows'))  42.3 us
    reduce_scatter x1, waiting for transfers between devices, body(): lax.psum_scatter(norm_terms, 'fsdp', scatter_dimension=0, tiled=True)  26.2 us
  transfers between devices with their start and end apart: 11, of which 8 were waited for; matrix products, arithmetic and copies ran while one was open for 6% of the time, Pallas kernels for 0%

commit v1 on v0

--- a/solution.py
+++ b/solution.py
@@ -3,6 +3,7 @@
 import jax.numpy as jnp
 from jax import lax
 from jax.sharding import PartitionSpec as P
+from jax.lax import axis_index, axis_size, ppermute
 
 KS = 7
 norm_eps = 1e-06
@@ -60,7 +61,26 @@
     scaled = (normed * norm_gain).astype(jnp.bfloat16)
     gathered = lax.all_gather(scaled, "fsdp", axis=0, tiled=True)
     up_full = lax.all_gather(w_up, ("dp", "rows"), axis=0, tiled=True)
-    down_full = lax.all_gather(w_down, ("dp", "rows"), axis=1, tiled=True)
+    carry_in, finding, step_out = (
+        axis_size(("dp", "rows")),
+        axis_index(("dp", "rows")),
+        w_down.shape[1],
+    )
+    seen_now, built = (w_down, 1)
+    while built < carry_in:
+        seen_now = jnp.concatenate(
+            [
+                seen_now,
+                ppermute(
+                    seen_now,
+                    axis_name=("dp", "rows"),
+                    perm=[(to_i, (to_i - built) % carry_in) for to_i in range(carry_in)],
+                ),
+            ],
+            axis=1,
+        )
+        built = 2 * built
+    down_full = jnp.roll(seen_now, finding * step_out, axis=1)
     hidden = jnp.dot(gathered, up_full, preferred_element_type=jnp.float32)
     active = gelu_exact(hidden).astype(jnp.bfloat16)
     mlp_terms = jnp.dot(active, down_full, preferred_element_type=jnp.float32)

time: 799 us -> 1040 us (1.30)
  waiting for transfers between devices: 625 us -> 811 us
  local copies, waits for them, and re-layouts: 12.1 us -> 60.1 us
  starting transfers between devices: 7.34 us -> 19.5 us
    ppermute x0 -> x4, waiting for transfers between devices: none -> 312 us  [body(): ppermute(seen_now, axis_name=('dp', 'rows'), perm=[(to_i, (to_i - built)...]
    all_gather x1 -> x0, waiting for transfers between devices: 73.7 us -> none  [body(): down_full = lax.all_gather(w_down, ('dp', 'rows'), axis=1, tiled=True)]
    all_gather x1, waiting for transfers between devices: 55.8 us -> 0.01 us  [body(): up_full = lax.all_gather(w_up, ('dp', 'rows'), axis=0, tiled=True)]
    another operation x50, local copies, waits for them, and re-layouts: 0.83 us -> 31 us  [body(): kernel_part = jnp.stack(kernel_rows).reshape(KS, KS, width)]
    unnamed x189 -> x222, local copies, waits for them, and re-layouts: 5.56 us -> 21.8 us
  transfers between devices with their start and end apart: 11 -> 14, of which waited for: 8 -> 9; matrix products, arithmetic and copies ran while one was open for 6% -> 6% of each run, Pallas kernels for 0% -> 0%
where the time goes in v1:
time: 1040 us
  waiting for transfers between devices  811 us (78%)
  blocking collectives  61 us (6%)
  local copies, waits for them, and re-layouts  60.1 us (6%)
  matrix products  42.4 us (4%)
  other arithmetic  33.4 us (3%)
  starting transfers between devices  19.5 us (2%)
  between operations  15.7 us (2%)
    ppermute x4, waiting for transfers between devices, body(): ppermute(seen_now, axis_name=('dp', 'rows'), perm=[(to_i, (to_i - built)...  312 us
    reduce_scatter x1, waiting for transfers between devices, body(): lax.psum_scatter(up_part, ('dp', 'rows'), scatter_dimension=0, tiled=True)  201 us
    reduce_scatter x1, waiting for transfers between devices, reduce_down(): lax.psum_scatter(down_part, ('dp', 'rows'), scatter_dimension=1, tiled=True)  199 us
    psum x1, waiting for transfers between devices, body(): lax.psum((kernel_part, gain_part, scale_part), ('dp', 'fsdp', 'rows'))  52.9 us
    psum x1, blocking collectives, body(): lax.psum((kernel_part, gain_part, scale_part), ('dp', 'fsdp', 'rows'))  39.8 us
    another operation x50, local copies, waits for them, and re-layouts, body(): kernel_part = jnp.stack(kernel_rows).reshape(KS, KS, width)  31 us
    reduce_scatter x1, waiting for transfers between devices, body(): lax.psum_scatter(norm_terms, 'fsdp', scatter_dimension=0, tiled=True)  26.2 us
    unnamed x222, local copies, waits for them, and re-layouts  21.8 us
  transfers between devices with their start and end apart: 14, of which 9 were waited for; matrix products, arithmetic and copies ran while one was open for 6% of the time, Pallas kernels for 0%

profile of v1, /device:TPU:0, one launch (start us, length us, event | category | flops | bytes accessed | tf_op | source)
XLA Modules:
  0.0 1043.0 jit_solution(13965752553437972903)
XLA Ops:
  7.2 0.7 all-gather.2.cloned.1.call-update
  8.0 5.5 collective-permute-start.2
  13.5 7.7 collective-permute-done.2
  21.2 1.4 pad_maximum_fusion.2
  23.1 41.9 %collective-permute-done.3 = bf16[3072,192]{0,1:T(8,128)(2,1)S(1)} collective-permute-done((bf16[3072,192]{0,1:T(8,128)(2,1)S(1)}, bf16[3072,192]{0,1:T(8,128)(2,1)S(1)}, u32[]{:S(2)}, u32[]{:S(2)}) %collective-permute-start.3) | collective-permute-done | bytes 1179680 | tf_op jit(solution)/shard_map/ppermute | solution.py:74
  65.3 3.0 collective-permute-start.4
  68.2 89.5 %collective-permute-done.4 = bf16[3072,384]{0,1:T(8,128)(2,1)S(1)} collective-permute-done((bf16[3072,384]{0,1:T(8,128)(2,1)S(1)}, bf16[3072,384]{0,1:T(8,128)(2,1)S(1)}, u32[]{:S(2)}, u32[]{:S(2)}) %collective-permute-start.4) | collective-permute-done | bytes 2359328 | tf_op jit(solution)/shard_map/ppermute | solution.py:74
  157.8 2.5 pad_maximum_fusion
  160.7 1.1 collective-permute-start.5
  161.8 1.3 collective-permute-start.1
  163.1 3.0 collective-permute-start
  167.0 0.9 slice_reduce_fusion.47
  168.0 0.8 constant_dynamic-update-slice_fusion.9
  169.0 9.5 fusion.117
  179.5 9.6 all_gather.9
  189.1 1.9 constant_dynamic-update-slice_fusion.8
  191.0 1.1 constant_dynamic-update-slice_fusion.7
  192.1 1.5 constant_dynamic-update-slice_fusion.6
  193.7 173.3 %collective-permute-done.5 = bf16[3072,768]{0,1:T(8,128)(2,1)} collective-permute-done((bf16[3072,768]{0,1:T(8,128)(2,1)}, bf16[3072,768]{0,1:T(8,128)(2,1)}, u32[]{:S(2)}, u32[]{:S(2)}) %collective-permute-start.5) | collective-permute-done | bytes 4718624 | tf_op jit(solution)/shard_map/ppermute | solution.py:74
  367.0 4.8 constant_dynamic-update-slice_fusion.5
  371.8 0.8 constant_dynamic-update-slice_fusion.4
  372.6 0.8 constant_dynamic-update-slice_fusion.3
  373.5 1.1 constant_dynamic-update-slice_fusion.2
  374.6 1.7 constant_dynamic-update-slice_fusion.1
  376.3 4.9 constant_dynamic-update-slice_fusion
  381.1 5.3 fusion.120
  386.5 1.6 copy-done.13
  388.1 7.9 fusion.14
  396.3 18.8 %reduce-scatter.5.cloned.1.call-done = bf16[128,1536]{1,0:T(8,128)(2,1)} async-done(((bf16[256,1536]{1,0:T(8,128)(2,1)}), bf16[128,1536]{1,0:T(8,128)(2,1)}) %reduce-scatter.5.cloned.1.call-update) | async-done | bytes 393232 | tf_op jit(solution)/shard_map/reduce_scatter | solution.py:87
  415.0 2.7 fusion.19
  417.7 11.6 %all_gather.11 = bf16[256,1536]{1,0:T(8,128)(2,1)S(1)} all-gather(bf16[128,1536]{1,0:T(8,128)(2,1)S(1)} %get-tuple-element.114), channel_id=1, replica_groups=mesh['dp'=4,'fsdp'=2,'rows'=4] {'fsdp'}, dimensions={0}, use_global_device_ids=true | all-gather | bytes 1179648 | tf_op jit(solution)/shard_map/all_gather | solution.py:95
  429.4 0.9 copy-done.11
  430.3 6.4 fusion.7
  436.7 1.2 copy-done.17
  437.9 3.8 fusion.121
  441.8 26.2 %reduce-scatter.7.cloned.1.call-done = f32[128,1536]{1,0:T(8,128)} async-done(((f32[256,1536]{1,0:T(8,128)}), f32[128,1536]{1,0:T(8,128)}) %reduce-scatter.7.cloned.1.call-update) | async-done | bytes 786448 | tf_op jit(solution)/shard_map/reduce_scatter | solution.py:107
  468.0 2.0 multiply_reduce_fusion
  470.0 3.6 multiply_reduce_fusion.2
  473.6 1.2 multiply_reduce_fusion.3
  474.8 2.0 multiply_reduce_fusion.1
  484.7 0.6 stack.169
  486.5 0.6 stack.172
  487.1 0.6 stack.173
  490.7 0.6 stack.179
  491.3 0.6 stack.180
  491.9 0.6 stack.181
  492.5 0.6 stack.182
  496.1 0.6 stack.188
  499.0 0.6 stack.193
  499.6 0.6 stack.194
  500.2 0.6 stack.195
  502.0 5.9 stack.199
  507.9 0.8 reshape.323
  508.8 8.0 fusion.122
  517.1 0.8 copy-done.12
  517.9 11.1 %fusion.116 = f32[3072,1536]{0,1:T(8,128)} fusion(bf16[256,1536]{1,0:T(8,128)(2,1)S(1)} %copy-done.12, f32[256,3072]{1,0:T(8,128)} %copy-done.13), kind=kOutput, calls=%fused_computation.332 | convolution fusion | flops 2419851264 | bytes 22806528 | tf_op jit(solution)/shard_map/dot_general | solution.py:96
  529.5 1.3 collective-permute-start.7
  530.8 3.0 collective-permute-start.6
  533.9 39.8 %all-reduce.2 = (f32[1536]{0:T(1024)}, f32[1536]{0:T(1024)}) all-reduce(f32[1536]{0:T(1024)} %get-tuple-element.56, f32[1536]{0:T(1024)} %get-tuple-element.113), channel_id=1, replica_groups=mesh['dp'=4,'fsdp'=2,'rows'=4] {'dp','fsdp','rows'}, use_global_device_ids=true, to_apply=%region_59.60 | all-reduce | flops 3072 | bytes 24576 | tf_op jit(solution)/shard_map/psum | solution.py:135
  574.2 7.5 fusion.107
  581.7 52.9 %all-reduce.5.cloned.1.call-done = f32[7,7,1536]{2,1,0:T(8,128)} async-done(((f32[7,7,1536]{2,1,0:T(8,128)}), f32[7,7,1536]{2,1,0:T(8,128)}) %all-reduce.5.cloned.1.call-update) | async-done | bytes 301072 | tf_op jit(solution)/shard_map/psum | solution.py:135
  634.6 200.8 %reduce-scatter.9.cloned.1.call-done = f32[96,3072]{1,0:T(8,128)} async-done(((f32[1536,3072]{1,0:T(8,128)}), f32[96,3072]{1,0:T(8,128)}) %reduce-scatter.9.cloned.1.call-update) | async-done | bytes 1179664 | tf_op jit(solution)/shard_map/reduce_scatter | solution.py:108
  835.4 199.0 %reduce-scatter.11.cloned.1.call-done = f32[3072,96]{0,1:T(8,128)} async-done(((f32[3072,1536]{0,1:T(8,128)}), f32[3072,96]{0,1:T(8,128)}) %reduce-scatter.11.cloned.1.call-update) | async-done | bytes 1179664 | tf_op jit(solution)/shard_map/reduce_scatter | solution.py:39
  1034.4 1.7 copy.24
  (280 shorter events, 22.4 us)
Async XLA Ops:
  7.2 57.9 %copy-start.4 = (bf16[3072,96]{0,1:T(8,128)(2,1)S(1)}, bf16[3072,96]{0,1:T(8,128)(2,1)}, u32[]{:S(2)}) copy-start(bf16[3072,96]{0,1:T(8,128)(2,1)} %param.11) | copy-start | bytes 1769476
  7.2 373.9 %all-gather.2.cloned.1.call-start = ((), (), s32[]{:S(2)}) async-start(), calls=%async_computation.4 | async-start | bytes 10027008 | tf_op jit(solution)/shard_map/all_gather | solution.py:63
  7.9 407.1 %reduce-scatter.5.cloned.1.call-start = ((), (), s32[]{:S(2)}) async-start(), calls=%async_computation.5 | async-start | bytes 1179648 | tf_op jit(solution)/shard_map/reduce_scatter | solution.py:87
  8.0 13.2 %collective-permute-start.2 = (bf16[3072,96]{0,1:T(8,128)(2,1)}, bf16[3072,96]{0,1:T(8,128)(2,1)S(1)}, u32[]{:S(2)}, u32[]{:S(2)}) collective-permute-start(bf16[3072,96]{0,1:T(8,128)(2,1)} %param.11), channel_id=1, source_target_pairs={{0,27},{1,0},{2,1},{3,2},{8,3},{9,8},{10,9},{11,10},{16,11},{17,16... | collective-permute-start | bytes 1769480 | tf_op jit(solution)/shard_map/ppermute | solution.py:74
  21.2 136.6 %copy-start.5 = (bf16[3072,96]{0,1:T(8,128)(2,1)}, bf16[3072,96]{0,1:T(8,128)(2,1)S(1)}, u32[]{:S(2)}) copy-start(bf16[3072,96]{0,1:T(8,128)(2,1)S(1)} %collective-permute-done.2) | copy-start | bytes 1769476
  22.6 42.5 %collective-permute-start.3 = (bf16[3072,192]{0,1:T(8,128)(2,1)S(1)}, bf16[3072,192]{0,1:T(8,128)(2,1)S(1)}, u32[]{:S(2)}, u32[]{:S(2)}) collective-permute-start(bf16[3072,192]{0,1:T(8,128)(2,1)S(1)} %pad_maximum_fusion.2), channel_id=1, source_target_pairs={{0,26},{1,27},{2,0},{3,1},{8,2},{9,3},{10,8},{11,9},{16,10},{17,11... | collective-permute-start | bytes 3538952 | tf_op jit(solution)/shard_map/ppermute | solution.py:74
  65.1 95.2 %copy-start.2 = (bf16[3072,192]{0,1:T(8,128)(2,1)}, bf16[3072,192]{0,1:T(8,128)(2,1)S(1)}, u32[]{:S(2)}) copy-start(bf16[3072,192]{0,1:T(8,128)(2,1)S(1)} %collective-permute-done.3) | copy-start | bytes 3538948
  65.2 96.5 %copy-start.7 = (bf16[1,4,32,1536]{3,2,1,0:T(8,128)(2,1)S(1)}, bf16[1,4,32,1536]{3,2,1,0:T(8,128)(2,1)}, u32[]{:S(2)}) copy-start(bf16[1,4,32,1536]{3,2,1,0:T(8,128)(2,1)} %param.7) | copy-start | bytes 1179652
  65.3 101.0 %copy-start.19 = (f32[7,7,1536]{2,1,0:T(8,128)S(1)}, f32[7,7,1536]{2,1,0:T(8,128)}, u32[]{:S(2)}) copy-start(f32[7,7,1536]{2,1,0:T(8,128)} %param.8) | copy-start | bytes 903172
  65.3 92.5 %collective-permute-start.4 = (bf16[3072,384]{0,1:T(8,128)(2,1)S(1)}, bf16[3072,384]{0,1:T(8,128)(2,1)S(1)}, u32[]{:S(2)}, u32[]{:S(2)}) collective-permute-start(bf16[3072,384]{0,1:T(8,128)(2,1)S(1)} %pad_maximum_fusion.1), channel_id=1, source_target_pairs={{0,24},{1,25},{2,26},{3,27},{8,0},{9,1},{10,2},{11,3},{16,8},{17,9... | collective-permute-start | bytes 7077896 | tf_op jit(solution)/shard_map/ppermute | solution.py:74
  160.7 206.3 %collective-permute-start.5 = (bf16[3072,768]{0,1:T(8,128)(2,1)}, bf16[3072,768]{0,1:T(8,128)(2,1)}, u32[]{:S(2)}, u32[]{:S(2)}) collective-permute-start(bf16[3072,768]{0,1:T(8,128)(2,1)} %pad_maximum_fusion), channel_id=1, source_target_pairs={{0,16},{1,17},{2,18},{3,19},{8,24},{9,25},{10,26},{11,27},{16,0},{... | collective-permute-start | bytes 14155784 | tf_op jit(solution)/shard_map/ppermute | solution.py:74
  161.8 7.0 collective-permute-start.1
  163.1 5.7 collective-permute-start
  193.7 179.0 %copy-start.6 = (bf16[3072,96]{0,1:T(8,128)(2,1)S(1)}, bf16[3072,96]{0,1:T(8,128)(2,1)}, u32[]{:S(2)}) copy-start(bf16[3072,96]{0,1:T(8,128)(2,1)} %copy-done.5) | copy-start | bytes 1769476
  396.0 71.9 %reduce-scatter.7.cloned.1.call-start = ((), (), s32[]{:S(2)}) async-start(), calls=%async_computation.6 | async-start | bytes 2359296 | tf_op jit(solution)/shard_map/reduce_scatter | solution.py:107
  437.9 30.1 %copy-start.100 = (f32[128]{0:T(128)S(1)}, f32[128]{0:T(128)}, u32[]{:S(2)}) copy-start(f32[128]{0:T(128)} %copy-done.99) | copy-start | bytes 1540
  437.9 30.1 %copy-start.102 = (f32[128]{0:T(128)S(1)}, f32[128]{0:T(128)}, u32[]{:S(2)}) copy-start(f32[128]{0:T(128)} %copy-done.101) | copy-start | bytes 1540
  441.7 192.9 %all-reduce.5.cloned.1.call-start = ((), (), s32[]{:S(2)}) async-start(), calls=%async_computation.9 | async-start | bytes 688128 | tf_op jit(solution)/shard_map/psum | solution.py:135
  474.8 34.0 %copy-start.10 = (bf16[256,1536]{1,0:T(8,128)(2,1)S(1)}, bf16[256,1536]{1,0:T(8,128)(2,1)}, u32[]{:S(2)}) copy-start(bf16[256,1536]{1,0:T(8,128)(2,1)} %all_gather.9) | copy-start | bytes 2359300
  476.8 32.0 %copy-start.18 = (bf16[256,3072]{1,0:T(8,128)(2,1)S(1)}, bf16[256,3072]{1,0:T(8,128)(2,1)}, u32[]{:S(2)}) copy-start(bf16[256,3072]{1,0:T(8,128)(2,1)} %copy-done.17) | copy-start | bytes 4718596
  508.7 326.6 %reduce-scatter.9.cloned.1.call-start = ((), (), s32[]{:S(2)}) async-start(), calls=%async_computation.7 | async-start | bytes 20054016 | tf_op jit(solution)/shard_map/reduce_scatter | solution.py:108
  516.8 517.6 %reduce-scatter.11.cloned.1.call-start = ((), (), s32[]{:S(2)}) async-start(), calls=%async_computation.8 | async-start | bytes 20054016 | tf_op jit(solution)/shard_map/reduce_scatter | solution.py:39
  529.0 44.8 %copy-start.16 = (bf16[1,4,32,1536]{3,2,1,0:T(8,128)(2,1)S(1)}, bf16[1,4,32,1536]{3,2,1,0:T(8,128)(2,1)}, u32[]{:S(2)}) copy-start(bf16[1,4,32,1536]{3,2,1,0:T(8,128)(2,1)} %param.13) | copy-start | bytes 1179652
  529.0 44.8 %copy-start.22 = (f32[1536]{0:T(1024)S(1)}, f32[1536]{0:T(1024)}, u32[]{:S(2)}) copy-start(f32[1536]{0:T(1024)} %copy-done.21) | copy-start | bytes 18436
  529.0 44.8 %copy-start.24 = (f32[1536]{0:T(1024)S(1)}, f32[1536]{0:T(1024)}, u32[]{:S(2)}) copy-start(f32[1536]{0:T(1024)} %copy-done.23) | copy-start | bytes 18436
  529.0 44.8 %copy-start.26 = (f32[1536]{0:T(1024)S(1)}, f32[1536]{0:T(1024)}, u32[]{:S(2)}) copy-start(f32[1536]{0:T(1024)} %copy-done.25) | copy-start | bytes 18436
  529.0 44.8 %copy-start.28 = (f32[1536]{0:T(1024)S(1)}, f32[1536]{0:T(1024)}, u32[]{:S(2)}) copy-start(f32[1536]{0:T(1024)} %copy-done.27) | copy-start | bytes 18436
  529.0 44.8 %copy-start.30 = (f32[1536]{0:T(1024)S(1)}, f32[1536]{0:T(1024)}, u32[]{:S(2)}) copy-start(f32[1536]{0:T(1024)} %copy-done.29) | copy-start | bytes 18436
  529.1 44.8 %copy-start.32 = (f32[1536]{0:T(1024)S(1)}, f32[1536]{0:T(1024)}, u32[]{:S(2)}) copy-start(f32[1536]{0:T(1024)} %copy-done.31) | copy-start | bytes 18436
  529.1 44.8 %copy-start.34 = (f32[1536]{0:T(1024)S(1)}, f32[1536]{0:T(1024)}, u32[]{:S(2)}) copy-start(f32[1536]{0:T(1024)} %copy-done.33) | copy-start | bytes 18436
  529.1 44.8 %copy-start.36 = (f32[1536]{0:T(1024)S(1)}, f32[1536]{0:T(1024)}, u32[]{:S(2)}) copy-start(f32[1536]{0:T(1024)} %copy-done.35) | copy-start | bytes 18436
  529.1 44.8 %copy-start.38 = (f32[1536]{0:T(1024)S(1)}, f32[1536]{0:T(1024)}, u32[]{:S(2)}) copy-start(f32[1536]{0:T(1024)} %copy-done.37) | copy-start | bytes 18436
  529.1 44.8 %copy-start.40 = (f32[1536]{0:T(1024)S(1)}, f32[1536]{0:T(1024)}, u32[]{:S(2)}) copy-start(f32[1536]{0:T(1024)} %copy-done.39) | copy-start | bytes 18436
  529.1 44.8 %copy-start.42 = (f32[1536]{0:T(1024)S(1)}, f32[1536]{0:T(1024)}, u32[]{:S(2)}) copy-start(f32[1536]{0:T(1024)} %copy-done.41) | copy-start | bytes 18436
  529.1 44.8 %copy-start.44 = (f32[1536]{0:T(1024)S(1)}, f32[1536]{0:T(1024)}, u32[]{:S(2)}) copy-start(f32[1536]{0:T(1024)} %copy-done.43) | copy-start | bytes 18436
  529.1 44.8 %copy-start.46 = (f32[1536]{0:T(1024)S(1)}, f32[1536]{0:T(1024)}, u32[]{:S(2)}) copy-start(f32[1536]{0:T(1024)} %copy-done.45) | copy-start | bytes 18436
  529.1 44.8 %copy-start.48 = (f32[1536]{0:T(1024)S(1)}, f32[1536]{0:T(1024)}, u32[]{:S(2)}) copy-start(f32[1536]{0:T(1024)} %copy-done.47) | copy-start | bytes 18436
  529.2 44.8 %copy-start.50 = (f32[1536]{0:T(1024)S(1)}, f32[1536]{0:T(1024)}, u32[]{:S(2)}) copy-start(f32[1536]{0:T(1024)} %copy-done.49) | copy-start | bytes 18436
  529.2 44.8 %copy-start.52 = (f32[1536]{0:T(1024)S(1)}, f32[1536]{0:T(1024)}, u32[]{:S(2)}) copy-start(f32[1536]{0:T(1024)} %copy-done.51) | copy-start | bytes 18436
  529.2 44.8 %copy-start.54 = (f32[1536]{0:T(1024)S(1)}, f32[1536]{0:T(1024)}, u32[]{:S(2)}) copy-start(f32[1536]{0:T(1024)} %copy-done.53) | copy-start | bytes 18436
  529.2 44.8 %copy-start.56 = (f32[1536]{0:T(1024)S(1)}, f32[1536]{0:T(1024)}, u32[]{:S(2)}) copy-start(f32[1536]{0:T(1024)} %copy-done.55) | copy-start | bytes 18436
  529.2 44.8 %copy-start.58 = (f32[1536]{0:T(1024)S(1)}, f32[1536]{0:T(1024)}, u32[]{:S(2)}) copy-start(f32[1536]{0:T(1024)} %copy-done.57) | copy-start | bytes 18436
  529.2 44.8 %copy-start.60 = (f32[1536]{0:T(1024)S(1)}, f32[1536]{0:T(1024)}, u32[]{:S(2)}) copy-start(f32[1536]{0:T(1024)} %copy-done.59) | copy-start | bytes 18436
  529.2 44.8 %copy-start.62 = (f32[1536]{0:T(1024)S(1)}, f32[1536]{0:T(1024)}, u32[]{:S(2)}) copy-start(f32[1536]{0:T(1024)} %copy-done.61) | copy-start | bytes 18436
  529.2 44.8 %copy-start.64 = (f32[1536]{0:T(1024)S(1)}, f32[1536]{0:T(1024)}, u32[]{:S(2)}) copy-start(f32[1536]{0:T(1024)} %copy-done.63) | copy-start | bytes 18436
  529.2 44.8 %copy-start.66 = (f32[1536]{0:T(1024)S(1)}, f32[1536]{0:T(1024)}, u32[]{:S(2)}) copy-start(f32[1536]{0:T(1024)} %copy-done.65) | copy-start | bytes 18436
  529.2 44.8 %copy-start.68 = (f32[1536]{0:T(1024)S(1)}, f32[1536]{0:T(1024)}, u32[]{:S(2)}) copy-start(f32[1536]{0:T(1024)} %copy-done.67) | copy-start | bytes 18436
  529.3 44.8 %copy-start.70 = (f32[1536]{0:T(1024)S(1)}, f32[1536]{0:T(1024)}, u32[]{:S(2)}) copy-start(f32[1536]{0:T(1024)} %copy-done.69) | copy-start | bytes 18436
  529.3 44.8 %copy-start.72 = (f32[1536]{0:T(1024)S(1)}, f32[1536]{0:T(1024)}, u32[]{:S(2)}) copy-start(f32[1536]{0:T(1024)} %copy-done.71) | copy-start | bytes 18436
  529.3 44.8 %copy-start.74 = (f32[1536]{0:T(1024)S(1)}, f32[1536]{0:T(1024)}, u32[]{:S(2)}) copy-start(f32[1536]{0:T(1024)} %copy-done.73) | copy-start | bytes 18436
  529.3 44.8 %copy-start.76 = (f32[1536]{0:T(1024)S(1)}, f32[1536]{0:T(1024)}, u32[]{:S(2)}) copy-start(f32[1536]{0:T(1024)} %copy-done.75) | copy-start | bytes 18436
  529.3 44.8 %copy-start.78 = (f32[1536]{0:T(1024)S(1)}, f32[1536]{0:T(1024)}, u32[]{:S(2)}) copy-start(f32[1536]{0:T(1024)} %copy-done.77) | copy-start | bytes 18436
  529.3 44.8 %copy-start.80 = (f32[1536]{0:T(1024)S(1)}, f32[1536]{0:T(1024)}, u32[]{:S(2)}) copy-start(f32[1536]{0:T(1024)} %copy-done.79) | copy-start | bytes 18436
  529.3 44.8 %copy-start.82 = (f32[1536]{0:T(1024)S(1)}, f32[1536]{0:T(1024)}, u32[]{:S(2)}) copy-start(f32[1536]{0:T(1024)} %copy-done.81) | copy-start | bytes 18436
  529.3 44.8 %copy-start.84 = (f32[1536]{0:T(1024)S(1)}, f32[1536]{0:T(1024)}, u32[]{:S(2)}) copy-start(f32[1536]{0:T(1024)} %copy-done.83) | copy-start | bytes 18436
  529.3 44.8 %copy-start.86 = (f32[1536]{0:T(1024)S(1)}, f32[1536]{0:T(1024)}, u32[]{:S(2)}) copy-start(f32[1536]{0:T(1024)} %copy-done.85) | copy-start | bytes 18436
  529.3 44.8 %copy-start.88 = (f32[1536]{0:T(1024)S(1)}, f32[1536]{0:T(1024)}, u32[]{:S(2)}) copy-start(f32[1536]{0:T(1024)} %copy-done.87) | copy-start | bytes 18436
  529.4 44.8 %copy-start.90 = (f32[1536]{0:T(1024)S(1)}, f32[1536]{0:T(1024)}, u32[]{:S(2)}) copy-start(f32[1536]{0:T(1024)} %copy-done.89) | copy-start | bytes 18436
  529.4 44.8 %copy-start.92 = (f32[1536]{0:T(1024)S(1)}, f32[1536]{0:T(1024)}, u32[]{:S(2)}) copy-start(f32[1536]{0:T(1024)} %copy-done.91) | copy-start | bytes 18436
  529.4 44.8 %copy-start.94 = (f32[1536]{0:T(1024)S(1)}, f32[1536]{0:T(1024)}, u32[]{:S(2)}) copy-start(f32[1536]{0:T(1024)} %copy-done.93) | copy-start | bytes 18436
  529.4 44.8 %copy-start.96 = (f32[1536]{0:T(1024)S(1)}, f32[1536]{0:T(1024)}, u32[]{:S(2)}) copy-start(f32[1536]{0:T(1024)} %copy-done.95) | copy-start | bytes 18436
  529.4 44.8 %copy-start.98 = (f32[1536]{0:T(1024)S(1)}, f32[1536]{0:T(1024)}, u32[]{:S(2)}) copy-start(f32[1536]{0:T(1024)} %copy-done.97) | copy-start | bytes 18436
  529.5 44.2 %collective-permute-start.7 = (bf16[1,3,32,1536]{3,2,1,0:T(8,128)(2,1)S(1)}, bf16[1,3,32,1536]{3,2,1,0:T(8,128)(2,1)S(1)}, u32[]{:S(2)}, u32[]{:S(2)}) collective-permute-start(bf16[1,3,32,1536]{3,2,1,0:T(8,128)(2,1)S(1)} %get-tuple-element.117), channel_id=1, source_target_pairs={{1,0},{2,1},{3,2},{5,4},{6,5},{7,6},{9,8},{10,9},{11,10},{13,12},{... | collective-permute-start | bytes 884744 | tf_op jit(solution)/shard_map/ppermute | solution.py:24
  530.8 42.9 %collective-permute-start.6 = (bf16[1,3,32,1536]{3,2,1,0:T(8,128)(2,1)S(1)}, bf16[1,3,32,1536]{3,2,1,0:T(8,128)(2,1)S(1)}, u32[]{:S(2)}, u32[]{:S(2)}) collective-permute-start(bf16[1,3,32,1536]{3,2,1,0:T(8,128)(2,1)S(1)} %get-tuple-element.116), channel_id=1, source_target_pairs={{0,1},{1,2},{2,3},{4,5},{5,6},{6,7},{8,9},{9,10},{10,11},{12,13},{... | collective-permute-start | bytes 884744 | tf_op jit(solution)/shard_map/ppermute | solution.py:23
  (56 other events, 631.7 us)
Sparse Core Ops, SparseCore 0:
  10.3 138.0 all-gather.1
  396.1 18.8 reduce-scatter.4
  441.8 26.0 reduce-scatter.6
  508.9 125.6 all-reduce.4
  639.7 195.6 reduce-scatter.8
  840.5 193.8 reduce-scatter.10
